TPU v7x, 32 devices: a whole 2x2x4 slice. The times are simulated.
32 devices in a mesh: dp: 4 (over y, x), seq: 8 (over z, core).
Axes of the slice: x: 2, y: 2, z: 4, core: 2. Of those that a mesh axis runs over, the one named last changes fastest.
Arguments:
- queries: bfloat16 [4, 8, 512, 2048], P('dp', 'seq'), may hold values from -48 to 48
- keys: bfloat16 [4, 8, 512, 2048], P('dp', 'seq'), may hold values from -6 to 6
- values: bfloat16 [4, 8, 512, 2048], P('dp', 'seq'), may hold values from -6 to 6
- out_grad: bfloat16 [4, 8, 512, 2048], P('dp', 'seq'), may hold values from -6 to 6
- out_weight: bfloat16 [2048, 2048], P('dp'), may hold values from -0.125 to 0.125
- row_mask: int32 [4, 4], replicated, may hold values from 0 to 1, as said below
- col_mask: int32 [8, 8], replicated, may hold values from 0 to 1, as said below
Outputs:
- layer_out: bfloat16 [4, 8, 512, 2048], P('dp', 'seq')
- query_grad: bfloat16 [4, 8, 512, 2048], P('dp', 'seq')
- key_grad: bfloat16 [4, 8, 512, 2048], P('dp', 'seq')
- value_grad: bfloat16 [4, 8, 512, 2048], P('dp', 'seq')
- wo_grad: float32 [2048, 2048], P(('dp', 'seq'))
Inputs may be any that keep to these rules, and one draw needn't show every extreme that they name: row_mask[a, b] is 1 for b = a and 0 for b > a. col_mask[r, s] is 1 for s = r and for s = r - 1, and 0 for s > r.
All inputs are finite; a program needn't handle non-finite values.
Results may differ from a plain program's by a relative error of at most 0.012.
Values may be sent and summed in bfloat16 or wider, within the bound.
No kernel may reach another device: no remote copies, remote signals or barrier semaphores. Data moves between devices by JAX's collectives and lax.ppermute only.
A program may use at most 192 MiB of HBM per device.

v0:
```python
import math
import jax
import jax.numpy as jnp
from jax import lax
from jax.sharding import PartitionSpec as P

DH = 128
COLS = 512
BLK = 128
masked_out = -1e30
scale = 1.0 / math.sqrt(DH)


def row_permit(row_mask):
    spread = jnp.repeat(jnp.repeat(row_mask, BLK, axis=0), BLK, axis=1)
    row_index = lax.broadcasted_iota(jnp.int32, (COLS, COLS), 0)
    col_index = lax.broadcasted_iota(jnp.int32, (COLS, COLS), 1)
    return (spread == 1) & (col_index <= row_index)


def softmax_parts(scores, allowed):
    highest = jnp.max(jnp.where(allowed, scores, masked_out), axis=-1, keepdims=True)
    attend = jnp.exp(jnp.where(allowed, scores - highest, masked_out))
    totals = jnp.sum(attend, axis=-1, keepdims=True)
    probs = (attend / totals).astype(jnp.bfloat16)
    return (probs, highest + jnp.log(totals))


def row_forward(q, k, v, allowed):
    scores = jnp.einsum("ihd,jhd->hij", q, k, preferred_element_type=jnp.float32) * scale
    probs, log_total = softmax_parts(scores, allowed[None])
    out = jnp.einsum("hij,jhd->ihd", probs, v, preferred_element_type=jnp.float32)
    return (out.astype(jnp.bfloat16), scores, log_total)


def row_backward(q, k, v, out, grad, scores, log_total, allowed):
    grad_dot = jnp.einsum("ihd,ihd->hi", grad, out, preferred_element_type=jnp.float32)
    back = jnp.where(allowed[None], jnp.exp(scores - log_total), 0.0)
    value_grad = jnp.einsum(
        "hij,ihd->jhd", back.astype(jnp.bfloat16), grad, preferred_element_type=jnp.float32
    )
    prob_grad = jnp.einsum("ihd,jhd->hij", grad, v, preferred_element_type=jnp.float32)
    score_grad = (back * (prob_grad - grad_dot[..., None])).astype(jnp.bfloat16)
    query_grad = jnp.einsum("hij,jhd->ihd", score_grad, k, preferred_element_type=jnp.float32)
    key_grad = jnp.einsum("hij,ihd->jhd", score_grad, q, preferred_element_type=jnp.float32)
    return tuple(
        (g.astype(jnp.bfloat16) for g in (query_grad * scale, key_grad * scale, value_grad))
    )


def column_forward(q, k, v, allowed):
    scores = jnp.einsum("rchd,schd->chrs", q, k, preferred_element_type=jnp.float32) * scale
    probs, log_total = softmax_parts(scores, allowed)
    out = jnp.einsum("chrs,schd->rchd", probs, v, preferred_element_type=jnp.float32)
    return (out.astype(jnp.bfloat16), scores, log_total)


def column_backward(q, k, v, out, grad, scores, log_total, allowed):
    grad_dot = jnp.einsum("rchd,rchd->chr", grad, out, preferred_element_type=jnp.float32)
    back = jnp.where(allowed, jnp.exp(scores - log_total), 0.0)
    value_grad = jnp.einsum(
        "chrs,rchd->schd", back.astype(jnp.bfloat16), grad, preferred_element_type=jnp.float32
    )
    prob_grad = jnp.einsum("rchd,schd->chrs", grad, v, preferred_element_type=jnp.float32)
    score_grad = (back * (prob_grad - grad_dot[..., None])).astype(jnp.bfloat16)
    query_grad = jnp.einsum("chrs,schd->rchd", score_grad, k, preferred_element_type=jnp.float32)
    key_grad = jnp.einsum("chrs,rchd->schd", score_grad, q, preferred_element_type=jnp.float32)
    return tuple(
        (g.astype(jnp.bfloat16) for g in (query_grad * scale, key_grad * scale, value_grad))
    )


def on_device(queries, keys, values, out_grad, out_weight, row_mask, col_mask):
    tokens, features = (queries.shape[2], queries.shape[3])
    half = features // 2
    heads_half = half // DH
    rows = lax.axis_size("seq")
    cols_each = tokens // rows
    weight = lax.all_gather(out_weight, "dp", axis=0, tiled=True)
    chunks = 2
    piece = cols_each // chunks

    def chunked(t):
        return t.reshape(rows, chunks, piece, half).transpose(1, 0, 2, 3)

    packed = jnp.stack([chunked(t[0, 0, :, half:]) for t in (queries, keys, values)], axis=1)
    col_ok = col_mask == 1
    shipped_all = [
        lax.all_to_all(packed[j], "seq", split_axis=1, concat_axis=1, tiled=True)
        for j in range(chunks)
    ]
    row_ok = row_permit(row_mask)
    split = lambda t: t[0, 0, :, :half].reshape(tokens, heads_half, DH)
    row_q, row_k, row_v = (split(queries), split(keys), split(values))
    row_out, row_scores, row_total = row_forward(row_q, row_k, row_v, row_ok)
    row_attn = row_out.reshape(tokens, half)
    flat_grad = out_grad[0, 0]
    contract = (((0,), (0,)), ((), ()))
    row_done, shipped_first = lax.optimization_barrier(
        ((row_out, row_scores, row_total), shipped_all[0])
    )
    row_out, row_scores, row_total = row_done
    row_attn = row_out.reshape(tokens, half)
    shipped_all[0] = shipped_first
    col_state = []
    col_back = []
    for j in range(chunks):
        shipped = shipped_all[j]
        col_q, col_k, col_v = (shipped[i].reshape(rows, piece, heads_half, DH) for i in range(3))
        col_out, col_scores, col_total = column_forward(col_q, col_k, col_v, col_ok)
        col_state.append((col_q, col_k, col_v, col_out, col_scores, col_total))
        col_back.append(col_out.reshape(rows, piece, half))
    col_attn = lax.all_to_all(
        jnp.stack(col_back, axis=1), "seq", split_axis=0, concat_axis=0, tiled=True
    ).reshape(tokens, half)
    attention = jnp.concatenate([row_attn, col_attn], axis=1)
    partial = lax.dot_general(attention, flat_grad, contract, preferred_element_type=jnp.float32)
    by_rows_of = (((1,), (1,)), ((), ()))
    row_grad = lax.dot_general(
        flat_grad, weight[:half], by_rows_of, preferred_element_type=jnp.float32
    ).astype(jnp.bfloat16)
    partial, late_weight = lax.optimization_barrier((partial, weight))
    col_grad = lax.dot_general(
        flat_grad, late_weight[half:], by_rows_of, preferred_element_type=jnp.float32
    ).astype(jnp.bfloat16)
    grad_col_part = chunked(col_grad)
    devices_all = lax.axis_size(("dp", "seq"))
    wo_grad = lax.psum_scatter(
        partial.astype(jnp.bfloat16), ("dp", "seq"), scatter_dimension=0, tiled=True
    ).astype(jnp.float32) * (1.0 / math.sqrt(tokens * devices_all))
    col_grads_back = []
    for j in range(chunks):
        grad_cols = lax.all_to_all(
            grad_col_part[j], "seq", split_axis=0, concat_axis=0, tiled=True
        ).reshape(rows, piece, heads_half, DH)
        col_q, col_k, col_v, col_out, col_scores, col_total = col_state[j]
        col_grads = column_backward(
            col_q, col_k, col_v, col_out, grad_cols, col_scores, col_total, col_ok
        )
        col_grads_back.append(
            lax.all_to_all(
                jnp.stack([g.reshape(rows, piece, half) for g in col_grads]),
                "seq",
                split_axis=1,
                concat_axis=1,
                tiled=True,
            )
        )
    col_grads_whole = jnp.stack(col_grads_back, axis=2).reshape(3, tokens, half)
    row_grads = row_backward(
        row_q,
        row_k,
        row_v,
        row_out,
        row_grad.reshape(tokens, heads_half, DH),
        row_scores,
        row_total,
        row_ok,
    )
    layer_out = jnp.dot(attention, weight, preferred_element_type=jnp.float32).astype(jnp.bfloat16)
    grads = [
        jnp.concatenate([row_grads[i].reshape(tokens, half), col_grads_whole[i]], axis=1)[
            None, None
        ]
        for i in range(3)
    ]
    return (layer_out[None, None], grads[0], grads[1], grads[2], wo_grad)


def solution(mesh):
    in_specs = (
        P("dp", "seq", None, None),
        P("dp", "seq", None, None),
        P("dp", "seq", None, None),
        P("dp", "seq", None, None),
        P("dp", None),
        P(),
        P(),
    )
    out_specs = (
        P("dp", "seq", None, None),
        P("dp", "seq", None, None),
        P("dp", "seq", None, None),
        P("dp", "seq", None, None),
        P(("dp", "seq"), None),
    )
    return jax.shard_map(
        on_device, mesh=mesh, in_specs=in_specs, out_specs=out_specs, check_vma=False
    )
```

profile of v0, /device:TPU:0, one launch (start us, length us, event | category | flops | bytes accessed | tf_op | source)
XLA Modules:
  0.0 367.7 jit_solution(15175648478473161992)
XLA Ops:
  15.7 6.3 %all-to-all-start.1 = ((bf16[3,8,32,1024]{3,2,0,1:T(8,128)(2,1)}), bf16[3,8,32,1024]{3,2,0,1:T(8,128)(2,1)}, u32[]{:S(2)}, u32[]{:S(2)}) async-start(bf16[3,8,32,1024]{3,2,0,1:T(8,128)(2,1)} %copy.219), calls=%async_computation.1 | async-start | bytes 3145728 | tf_op jit(solution)/shard_map/all_to_all | solution.py:89
  30.7 29.2 %all-to-all-done.1 = bf16[3,8,32,1024]{3,2,0,1:T(8,128)(2,1)} async-done(((bf16[3,8,32,1024]{3,2,0,1:T(8,128)(2,1)}), bf16[3,8,32,1024]{3,2,0,1:T(8,128)(2,1)}, u32[]{:S(2)}, u32[]{:S(2)}) %all-to-all-start.1) | async-done | bytes 1572896 | tf_op jit(solution)/shard_map/all_to_all | solution.py:89
  59.9 4.6 %all-to-all-start = ((bf16[3,8,32,1024]{3,2,0,1:T(8,128)(2,1)}), bf16[3,8,32,1024]{3,2,0,1:T(8,128)(2,1)}, u32[]{:S(2)}, u32[]{:S(2)}) async-start(bf16[3,8,32,1024]{3,2,0,1:T(8,128)(2,1)} %copy.211), calls=%async_computation | async-start | bytes 3145728 | tf_op jit(solution)/shard_map/all_to_all | solution.py:89
  64.5 2.9 select_reduce_fusion
  70.7 3.6 fusion.36
  78.5 23.8 %all-to-all-done = bf16[3,8,32,1024]{3,2,0,1:T(8,128)(2,1)} async-done(((bf16[3,8,32,1024]{3,2,0,1:T(8,128)(2,1)}), bf16[3,8,32,1024]{3,2,0,1:T(8,128)(2,1)}, u32[]{:S(2)}, u32[]{:S(2)}) %all-to-all-start) | async-done | bytes 1572896 | tf_op jit(solution)/shard_map/all_to_all | solution.py:89
  121.2 4.2 %all-to-all-start.2 = ((bf16[8,2,32,1024]{3,2,1,0:T(8,128)(2,1)}), bf16[8,2,32,1024]{3,2,1,0:T(8,128)(2,1)}, u32[]{:S(2)}, u32[]{:S(2)}) async-start(bf16[8,2,32,1024]{3,2,1,0:T(8,128)(2,1)} %copy.225), calls=%async_computation.2 | async-start | bytes 2097152 | tf_op jit(solution)/shard_map/all_to_all | solution.py:113
  128.3 23.7 %all-to-all-done.2 = bf16[8,2,32,1024]{3,2,1,0:T(8,128)(2,1)} async-done(((bf16[8,2,32,1024]{3,2,1,0:T(8,128)(2,1)}), bf16[8,2,32,1024]{3,2,1,0:T(8,128)(2,1)}, u32[]{:S(2)}, u32[]{:S(2)}) %all-to-all-start.2) | async-done | bytes 1048608 | tf_op jit(solution)/shard_map/all_to_all | solution.py:113
  154.3 8.3 %fusion.14 = bf16[2048,2048]{1,0:T(8,128)(2,1)} fusion(bf16[1,1,512,2048]{3,2,1,0:T(8,128)(2,1)S(1)} %copy-done, bf16[512,1024]{0,1:T(8,128)(2,1)} %copy.226, bf16[512,1024]{0,1:T(8,128)(2,1)} %bitcast.241), kind=kOutput, calls=%fused_computation.29 | convolution fusion | flops 4299161600 | bytes 12582912 | tf_op jit(solution)/shard_map/dot_general | solution.py:117
  162.6 4.5 %fusion.18 = bf16[1024,512]{0,1:T(8,128)(2,1)S(1)} fusion(bf16[1,1,512,2048]{3,2,1,0:T(8,128)(2,1)S(1)} %copy-done, bf16[2048,2048]{1,0:T(8,128)(2,1)} %all-gather.2.cloned.1.call-done), kind=kOutput, calls=%fused_computation.42 | convolution fusion | flops 2148007936 | bytes 7340032 | tf_op jit(solution)/shard_map/dot_general | solution.py:123
  168.4 4.2 %all-to-all-start.3 = ((bf16[8,32,1024]{2,1,0:T(8,128)(2,1)}), bf16[8,32,1024]{2,1,0:T(8,128)(2,1)}, u32[]{:S(2)}, u32[]{:S(2)}) async-start(bf16[8,32,1024]{2,1,0:T(8,128)(2,1)} %get-tuple-element.37), calls=%async_computation.3 | async-start | bytes 1048576 | tf_op jit(solution)/shard_map/all_to_all | solution.py:133
  174.3 20.8 %all-to-all-done.3 = bf16[8,32,1024]{2,1,0:T(8,128)(2,1)} async-done(((bf16[8,32,1024]{2,1,0:T(8,128)(2,1)}), bf16[8,32,1024]{2,1,0:T(8,128)(2,1)}, u32[]{:S(2)}, u32[]{:S(2)}) %all-to-all-start.3) | async-done | bytes 524320 | tf_op jit(solution)/shard_map/all_to_all | solution.py:133
  195.1 4.2 %all-to-all-start.5 = ((bf16[8,32,1024]{2,1,0:T(8,128)(2,1)}), bf16[8,32,1024]{2,1,0:T(8,128)(2,1)}, u32[]{:S(2)}, u32[]{:S(2)}) async-start(bf16[8,32,1024]{2,1,0:T(8,128)(2,1)} %get-tuple-element.36), calls=%async_computation.5 | async-start | bytes 1048576 | tf_op jit(solution)/shard_map/all_to_all | solution.py:133
  223.0 4.5 %all-to-all-start.4 = ((bf16[3,8,32,1024]{3,2,0,1:T(8,128)(2,1)}), bf16[3,8,32,1024]{3,2,0,1:T(8,128)(2,1)}, u32[]{:S(2)}, u32[]{:S(2)}) async-start(bf16[3,8,32,1024]{3,2,0,1:T(8,128)(2,1)} %copy.242), calls=%async_computation.4 | async-start | bytes 3145728 | tf_op jit(solution)/shard_map/all_to_all | solution.py:141
  227.5 4.6 %fusion.31 = bf16[64,8,8,128]{3,1,2,0:T(8,128)(2,1)S(1)} fusion(bf16[2048,2048]{1,0:T(8,128)(2,1)} %all-gather.2.cloned.1.call-done, bf16[1,1,512,2048]{3,2,1,0:T(8,128)(2,1)S(1)} %copy-done), kind=kOutput, calls=%fused_computation.45 | convolution fusion | flops 2148007936 | bytes 7340032 | tf_op jit(solution)/shard_map/dot_general | solution.py:119
  256.5 26.0 %all-to-all-done.4 = bf16[3,8,32,1024]{3,2,0,1:T(8,128)(2,1)} async-done(((bf16[3,8,32,1024]{3,2,0,1:T(8,128)(2,1)}), bf16[3,8,32,1024]{3,2,0,1:T(8,128)(2,1)}, u32[]{:S(2)}, u32[]{:S(2)}) %all-to-all-start.4) | async-done | bytes 1572896 | tf_op jit(solution)/shard_map/all_to_all | solution.py:141
  282.4 5.8 %all-to-all-start.6 = ((bf16[3,8,32,1024]{3,2,0,1:T(8,128)(2,1)}), bf16[3,8,32,1024]{3,2,0,1:T(8,128)(2,1)}, u32[]{:S(2)}, u32[]{:S(2)}) async-start(bf16[3,8,32,1024]{3,2,0,1:T(8,128)(2,1)} %copy.254), calls=%async_computation.6 | async-start | bytes 3145728 | tf_op jit(solution)/shard_map/all_to_all | solution.py:141
  288.3 5.5 %multiply_convert_fusion = bf16[8,512,512]{1,2,0:T(8,128)(2,1)S(1)} fusion(f32[8,512,512]{1,2,0:T(8,128)} %copy-done.1, f32[8,512]{1,0:T(8,128)S(1)} %multiply_reduce_fusion, f32[8,512]{1,0:T(8,128)S(1)} %bitcast.246, pred[512,512]{0,1:T(8,128)(4,1)S(1)} %fusion.53, bf16[512,8,128]{0,2,1:T(8,128)(2,1)} %copy.259, bf16[512,8,128]{0,2,1:T(8,128)(2,1)S(1)} %bitcast.214), kind=kOutput, calls=%fused_computation | convolution fusion | flops 547356672 | bytes 14974976 | tf_op jit(solution)/shard_map/ihd,jhd->hij/dot_general | solution.py:42
  297.2 5.1 %multiply_convert_fusion.1 = bf16[8,512,128]{1,2,0:T(8,128)(2,1)} fusion(bf16[8,512,512]{1,2,0:T(8,128)(2,1)} %copy-done.2, bf16[512,8,128]{0,2,1:T(8,128)(2,1)} %bitcast.224), kind=kOutput, calls=%fused_computation.33 | convolution fusion | flops 537919488 | bytes 6291456 | tf_op jit(solution)/shard_map/hij,ihd->jhd/dot_general | solution.py:45
  304.6 6.0 %fusion.28 = bf16[8,128,512]{2,1,0:T(8,128)(2,1)} fusion(bf16[512,8,128]{0,2,1:T(8,128)(2,1)S(1)} %copy-done.20, f32[8,512,512]{1,2,0:T(8,128)} %copy-done.1, f32[8,512]{1,0:T(8,128)S(1)} %bitcast.247, pred[512,512]{0,1:T(8,128)(4,1)S(1)} %fusion.53), kind=kOutput, calls=%fused_computation.44 | convolution fusion | flops 543686656 | bytes 10764288 | tf_op jit(solution)/shard_map/hij,ihd->jhd/dot_general | solution.py:39
  312.1 10.0 %fusion.12 = bf16[1,1,512,2048]{3,2,1,0:T(8,128)(2,1)} fusion(bf16[2048,2048]{1,0:T(8,128)(2,1)} %all-gather.2.cloned.1.call-done, bf16[512,1024]{0,1:T(8,128)(2,1)} %copy.226, bf16[512,1024]{0,1:T(8,128)(2,1)} %bitcast.242), kind=kOutput, calls=%fused_computation.23 | convolution fusion | flops 4300210176 | bytes 12582912 | tf_op jit(solution)/shard_map/dot_general | solution.py:160
  322.0 2.8 copy.356
  324.8 19.7 %all-to-all-done.6 = bf16[3,8,32,1024]{3,2,0,1:T(8,128)(2,1)} async-done(((bf16[3,8,32,1024]{3,2,0,1:T(8,128)(2,1)}), bf16[3,8,32,1024]{3,2,0,1:T(8,128)(2,1)}, u32[]{:S(2)}, u32[]{:S(2)}) %all-to-all-start.6) | async-done | bytes 1572896 | tf_op jit(solution)/shard_map/all_to_all | solution.py:141
  351.2 7.6 %reduce-scatter.2.cloned.1.call-done = bf16[64,2048]{1,0:T(8,128)(2,1)} async-done(((bf16[2048,2048]{1,0:T(8,128)(2,1)}), bf16[64,2048]{1,0:T(8,128)(2,1)}) %reduce-scatter.2.cloned.1.call-update) | async-done | bytes 262160 | tf_op jit(solution)/shard_map/reduce_scatter | solution.py:128
  (181 shorter events, 114.9 us)
Async XLA Ops:
  7.2 147.1 %copy-start = (bf16[1,1,512,2048]{3,2,1,0:T(8,128)(2,1)S(1)}, bf16[1,1,512,2048]{3,2,1,0:T(8,128)(2,1)}, u32[]{:S(2)}) copy-start(bf16[1,1,512,2048]{3,2,1,0:T(8,128)(2,1)} %param.10) | copy-start | bytes 6291460
  7.2 155.4 %all-gather.2.cloned.1.call-start = ((), (), s32[]{:S(2)}) async-start(), calls=%async_computation.8 | async-start | bytes 10485760 | tf_op jit(solution)/shard_map/all_gather | solution.py:79
  14.3 7.6 %copy-start.43 = (s32[4,4]{1,0:T(4,128)S(1)}, s32[4,4]{1,0:T(4,128)}, u32[]{:S(2)}) copy-start(s32[4,4]{1,0:T(4,128)} %param.12) | copy-start | bytes 196
  14.4 7.8 %copy-start.42 = (s32[8,8]{1,0:T(8,128)S(1)}, s32[8,8]{1,0:T(8,128)}, u32[]{:S(2)}) copy-start(s32[8,8]{1,0:T(8,128)} %param.13) | copy-start | bytes 772
  15.7 44.3 %all-to-all-start.1 = ((bf16[3,8,32,1024]{3,2,0,1:T(8,128)(2,1)}), bf16[3,8,32,1024]{3,2,0,1:T(8,128)(2,1)}, u32[]{:S(2)}, u32[]{:S(2)}) async-start(bf16[3,8,32,1024]{3,2,0,1:T(8,128)(2,1)} %copy.219), calls=%async_computation.1 | async-start | bytes 3145728 | tf_op jit(solution)/shard_map/all_to_all | solution.py:89
  22.2 186.8 %copy-start.39 = (pred[8,8]{0,1:T(8,128)(4,1)}, pred[8,8]{0,1:T(8,128)(4,1)S(1)}, u32[]{:S(2)}) copy-start(pred[8,8]{0,1:T(8,128)(4,1)S(1)} %copy.213) | copy-start | bytes 196
  25.3 39.2 %copy-start.5 = (bf16[1,1,512,1024]{2,3,1,0:T(8,128)(2,1)}, bf16[1,1,512,1024]{2,3,1,0:T(8,128)(2,1)S(1)}, u32[]{:S(2)}) copy-start(bf16[1,1,512,1024]{2,3,1,0:T(8,128)(2,1)S(1)} %copy.296) | copy-start | bytes 3145732
  59.9 42.4 %all-to-all-start = ((bf16[3,8,32,1024]{3,2,0,1:T(8,128)(2,1)}), bf16[3,8,32,1024]{3,2,0,1:T(8,128)(2,1)}, u32[]{:S(2)}, u32[]{:S(2)}) async-start(bf16[3,8,32,1024]{3,2,0,1:T(8,128)(2,1)} %copy.211), calls=%async_computation | async-start | bytes 3145728 | tf_op jit(solution)/shard_map/all_to_all | solution.py:89
  105.0 3.5 copy-start.31
  105.9 7.0 %copy-start.37 = (f32[32,8,8]{2,1,0:T(8,128)}, f32[32,8,8]{2,1,0:T(8,128)S(1)}, u32[]{:S(2)}) copy-start(f32[32,8,8]{2,1,0:T(8,128)S(1)} %get-tuple-element.40) | copy-start | bytes 24580
  121.2 30.8 %all-to-all-start.2 = ((bf16[8,2,32,1024]{3,2,1,0:T(8,128)(2,1)}), bf16[8,2,32,1024]{3,2,1,0:T(8,128)(2,1)}, u32[]{:S(2)}, u32[]{:S(2)}) async-start(bf16[8,2,32,1024]{3,2,1,0:T(8,128)(2,1)} %copy.225), calls=%async_computation.2 | async-start | bytes 2097152 | tf_op jit(solution)/shard_map/all_to_all | solution.py:113
  125.4 233.4 %reduce-scatter.2.cloned.1.call-start = ((), (), s32[]{:S(2)}) async-start(), calls=%async_computation.9 | async-start | bytes 8650752 | tf_op jit(solution)/shard_map/reduce_scatter | solution.py:128
  168.4 26.7 %all-to-all-start.3 = ((bf16[8,32,1024]{2,1,0:T(8,128)(2,1)}), bf16[8,32,1024]{2,1,0:T(8,128)(2,1)}, u32[]{:S(2)}, u32[]{:S(2)}) async-start(bf16[8,32,1024]{2,1,0:T(8,128)(2,1)} %get-tuple-element.37), calls=%async_computation.3 | async-start | bytes 1048576 | tf_op jit(solution)/shard_map/all_to_all | solution.py:133
  195.1 27.9 %all-to-all-start.5 = ((bf16[8,32,1024]{2,1,0:T(8,128)(2,1)}), bf16[8,32,1024]{2,1,0:T(8,128)(2,1)}, u32[]{:S(2)}, u32[]{:S(2)}) async-start(bf16[8,32,1024]{2,1,0:T(8,128)(2,1)} %get-tuple-element.36), calls=%async_computation.5 | async-start | bytes 1048576 | tf_op jit(solution)/shard_map/all_to_all | solution.py:133
  206.0 4.7 %copy-start.26 = (bf16[32,8,8,128]{3,2,1,0:T(8,128)(2,1)S(1)}, bf16[32,8,8,128]{3,2,1,0:T(8,128)(2,1)}, u32[]{:S(2)}) copy-start(bf16[32,8,8,128]{3,2,1,0:T(8,128)(2,1)} %copy-done.25) | copy-start | bytes 1572868
  223.0 59.4 %all-to-all-start.4 = ((bf16[3,8,32,1024]{3,2,0,1:T(8,128)(2,1)}), bf16[3,8,32,1024]{3,2,0,1:T(8,128)(2,1)}, u32[]{:S(2)}, u32[]{:S(2)}) async-start(bf16[3,8,32,1024]{3,2,0,1:T(8,128)(2,1)} %copy.242), calls=%async_computation.4 | async-start | bytes 3145728 | tf_op jit(solution)/shard_map/all_to_all | solution.py:141
  235.8 4.3 %copy-start.40 = (pred[8,8]{0,1:T(8,128)(4,1)S(1)}, pred[8,8]{0,1:T(8,128)(4,1)}, u32[]{:S(2)}) copy-start(pred[8,8]{0,1:T(8,128)(4,1)} %copy-done.39) | copy-start | bytes 196
  243.7 4.7 %copy-start.17 = (bf16[32,8,8,128]{3,2,1,0:T(8,128)(2,1)S(1)}, bf16[32,8,8,128]{3,2,1,0:T(8,128)(2,1)}, u32[]{:S(2)}) copy-start(bf16[32,8,8,128]{3,2,1,0:T(8,128)(2,1)} %copy.304) | copy-start | bytes 1572868
  248.4 3.5 copy-start.15
  255.1 33.1 %copy-start.19 = (bf16[1,1,512,1024]{2,3,1,0:T(8,128)(2,1)S(1)}, bf16[1,1,512,1024]{2,3,1,0:T(8,128)(2,1)}, u32[]{:S(2)}) copy-start(bf16[1,1,512,1024]{2,3,1,0:T(8,128)(2,1)} %copy.297) | copy-start | bytes 3145732
  255.1 33.1 %copy-start.38 = (f32[8,512,1]{1,0,2:T(8,128)S(1)}, f32[8,512,1]{1,0,2:T(8,128)}, u32[]{:S(2)}) copy-start(f32[8,512,1]{1,0,2:T(8,128)} %add_bitcast_fusion) | copy-start | bytes 49156
  282.4 62.1 %all-to-all-start.6 = ((bf16[3,8,32,1024]{3,2,0,1:T(8,128)(2,1)}), bf16[3,8,32,1024]{3,2,0,1:T(8,128)(2,1)}, u32[]{:S(2)}, u32[]{:S(2)}) async-start(bf16[3,8,32,1024]{3,2,0,1:T(8,128)(2,1)} %copy.254), calls=%async_computation.6 | async-start | bytes 3145728 | tf_op jit(solution)/shard_map/all_to_all | solution.py:141
  288.3 5.6 %copy-start.6 = (bf16[1,1,512,1024]{2,3,1,0:T(8,128)(2,1)S(1)}, bf16[1,1,512,1024]{2,3,1,0:T(8,128)(2,1)}, u32[]{:S(2)}) copy-start(bf16[1,1,512,1024]{2,3,1,0:T(8,128)(2,1)} %copy-done.5) | copy-start | bytes 3145732
  297.2 7.3 %copy-start.20 = (bf16[512,8,128]{0,2,1:T(8,128)(2,1)S(1)}, bf16[512,8,128]{0,2,1:T(8,128)(2,1)}, u32[]{:S(2)}) copy-start(bf16[512,8,128]{0,2,1:T(8,128)(2,1)} %copy.259) | copy-start | bytes 3145732
  (29 other events, 58.2 us)
Sparse Core Ops, SparseCore 0:
  9.9 90.2 all-gather.1
  162.8 196.0 reduce-scatter.1
where the time goes:
time: 372 us; the launch traced here: 368 us
  waiting for transfers between devices  153 us (41%)
  local copies, waits for them, and re-layouts  75.6 us (20%)
  matrix products  65.5 us (18%)
  starting transfers between devices  34.4 us (9%)
  other arithmetic  24.4 us (7%)
  between operations  15 us (4%)
    all_to_all x2, waiting for transfers between devices, on_device(): lax.all_to_all(packed[j], 'seq', split_axis=1, concat_axis=1, tiled=True)  53 us
    all_to_all x2, waiting for transfers between devices, on_device(): lax.all_to_all(jnp.stack([g.reshape(rows, piece, half) for g in col_grads...  45.6 us
    all_to_all x1, waiting for transfers between devices, on_device(): lax.all_to_all(jnp.stack(col_back, axis=1), 'seq', split_axis=0, concat_a...  23.7 us
    all_to_all x2, waiting for transfers between devices, on_device(): lax.all_to_all(grad_col_part[j], 'seq', split_axis=0, concat_axis=0, tile...  22.1 us
    unnamed x102, local copies, waits for them, and re-layouts  20.3 us
    another operation x8, local copies, waits for them, and re-layouts, on_device(): jnp.stack([g.reshape(rows, piece, half) for g in col_grads])  13.2 us
    all_to_all x2, starting transfers between devices, on_device(): lax.all_to_all(packed[j], 'seq', split_axis=1, concat_axis=1, tiled=True)  10.9 us
    all_to_all x2, starting transfers between devices, on_device(): lax.all_to_all(jnp.stack([g.reshape(rows, piece, half) for g in col_grads...  10.3 us
  transfers between devices with their start and end apart: 9, of which 8 were waited for; matrix products, arithmetic and copies ran while one was open for 43% of the time, Pallas kernels for 0%

commit v1 on v0

--- a/solution.py
+++ b/solution.py
@@ -138,12 +138,20 @@
             col_q, col_k, col_v, col_out, grad_cols, col_scores, col_total, col_ok
         )
         col_grads_back.append(
-            lax.all_to_all(
-                jnp.stack([g.reshape(rows, piece, half) for g in col_grads]),
-                "seq",
-                split_axis=1,
-                concat_axis=1,
-                tiled=True,
+            jnp.concatenate(
+                lax.all_to_all(
+                    jnp.stack(
+                        jnp.split(
+                            jnp.stack([g.reshape(rows, piece, half) for g in col_grads]),
+                            lax.axis_size("seq"),
+                            axis=1,
+                        )
+                    ),
+                    "seq",
+                    0,
+                    0,
+                ),
+                axis=1,
             )
         )
     col_grads_whole = jnp.stack(col_grads_back, axis=2).reshape(3, tokens, half)

time: 372 us -> 383 us (1.030)
  waiting for transfers between devices: 153 us -> 175 us
  other arithmetic: 24.4 us -> 20 us
    all_to_all x2, waiting for transfers between devices: 45.6 us -> 62.3 us  [on_device(): lax.all_to_all(jnp.stack(jnp.split(jnp.stack([g.reshape(rows, piece, half...]
    all_to_all x2, waiting for transfers between devices: 22.1 us -> 35 us  [on_device(): lax.all_to_all(grad_col_part[j], 'seq', split_axis=0, concat_axis=0, tile...]
    unnamed x102 -> x118, local copies, waits for them, and re-layouts: 20.3 us -> 30.4 us
    reduce_scatter x1, waiting for transfers between devices: 7.6 us -> 0.01 us  [on_device(): lax.psum_scatter(partial.astype(jnp.bfloat16), ('dp', 'seq'), scatter_dim...]
    another operation x8 -> x7, local copies, waits for them, and re-layouts: 13.2 us -> 6.9 us  [on_device(): jnp.stack([g.reshape(rows, piece, half) for g in col_grads])]
    all_to_all x2 -> x0, local copies, waits for them, and re-layouts: 4.42 us -> none  [on_device(): lax.all_to_all(jnp.stack([g.reshape(rows, piece, half) for g in col_grads...]
  transfers between devices with their start and end apart: 9 -> 9, of which waited for: 8 -> 7; matrix products, arithmetic and copies ran while one was open for 43% -> 38% of each run, Pallas kernels for 0% -> 0%
where the time goes in v1:
time: 383 us; the launch traced here: 379 us
  waiting for transfers between devices  175 us (46%)
  local copies, waits for them, and re-layouts  72 us (19%)
  matrix products  61.7 us (16%)
  starting transfers between devices  34.9 us (9%)
  other arithmetic  20 us (5%)
  between operations  15 us (4%)
    all_to_all x2, waiting for transfers between devices, on_device(): lax.all_to_all(jnp.stack(jnp.split(jnp.stack([g.reshape(rows, piece, half...  62.3 us
    all_to_all x2, waiting for transfers between devices, on_device(): lax.all_to_all(packed[j], 'seq', split_axis=1, concat_axis=1, tiled=True)  53.1 us
    all_to_all x2, waiting for transfers between devices, on_device(): lax.all_to_all(grad_col_part[j], 'seq', split_axis=0, concat_axis=0, tile...  35 us
    unnamed x118, local copies, waits for them, and re-layouts  30.4 us
    all_to_all x1, waiting for transfers between devices, on_device(): lax.all_to_all(jnp.stack(col_back, axis=1), 'seq', split_axis=0, concat_a...  24.1 us
    all_to_all x2, starting transfers between devices, on_device(): lax.all_to_all(packed[j], 'seq', split_axis=1, concat_axis=1, tiled=True)  11.2 us
    all_to_all x2, starting transfers between devices, on_device(): lax.all_to_all(jnp.stack(jnp.split(jnp.stack([g.reshape(rows, piece, half...  10.9 us
    dot_general x1, matrix products, on_device(): jnp.dot(attention, weight, preferred_element_type=jnp.float32)  9.63 us
  transfers between devices with their start and end apart: 9, of which 7 were waited for; matrix products, arithmetic and copies ran while one was open for 38% of the time, Pallas kernels for 0%

profile of v1, /device:TPU:0, one launch (start us, length us, event | category | flops | bytes accessed | tf_op | source)
XLA Modules:
  0.0 378.8 jit_solution(5496500957778373669)
XLA Ops:
  16.5 6.5 %all-to-all-start.1 = ((bf16[3,8,32,1024]{3,2,0,1:T(8,128)(2,1)}), bf16[3,8,32,1024]{3,2,0,1:T(8,128)(2,1)}, u32[]{:S(2)}, u32[]{:S(2)}) async-start(bf16[3,8,32,1024]{3,2,0,1:T(8,128)(2,1)} %copy.256), calls=%async_computation.1 | async-start | bytes 3145728 | tf_op jit(solution)/shard_map/all_to_all | solution.py:89
  28.8 2.7 copy.248
  31.6 29.3 %all-to-all-done.1 = bf16[3,8,32,1024]{3,2,0,1:T(8,128)(2,1)} async-done(((bf16[3,8,32,1024]{3,2,0,1:T(8,128)(2,1)}), bf16[3,8,32,1024]{3,2,0,1:T(8,128)(2,1)}, u32[]{:S(2)}, u32[]{:S(2)}) %all-to-all-start.1) | async-done | bytes 1572896 | tf_op jit(solution)/shard_map/all_to_all | solution.py:89
  60.9 4.8 %all-to-all-start = ((bf16[3,8,32,1024]{3,2,0,1:T(8,128)(2,1)}), bf16[3,8,32,1024]{3,2,0,1:T(8,128)(2,1)}, u32[]{:S(2)}, u32[]{:S(2)}) async-start(bf16[3,8,32,1024]{3,2,0,1:T(8,128)(2,1)} %copy.248), calls=%async_computation | async-start | bytes 3145728 | tf_op jit(solution)/shard_map/all_to_all | solution.py:89
  65.7 2.9 select_reduce_fusion
  71.8 3.6 fusion.36
  79.7 23.8 %all-to-all-done = bf16[3,8,32,1024]{3,2,0,1:T(8,128)(2,1)} async-done(((bf16[3,8,32,1024]{3,2,0,1:T(8,128)(2,1)}), bf16[3,8,32,1024]{3,2,0,1:T(8,128)(2,1)}, u32[]{:S(2)}, u32[]{:S(2)}) %all-to-all-start) | async-done | bytes 1572896 | tf_op jit(solution)/shard_map/all_to_all | solution.py:89
  122.6 4.2 %all-to-all-start.2 = ((bf16[8,2,32,1024]{3,2,1,0:T(8,128)(2,1)}), bf16[8,2,32,1024]{3,2,1,0:T(8,128)(2,1)}, u32[]{:S(2)}, u32[]{:S(2)}) async-start(bf16[8,2,32,1024]{3,2,1,0:T(8,128)(2,1)} %copy.262), calls=%async_computation.2 | async-start | bytes 2097152 | tf_op jit(solution)/shard_map/all_to_all | solution.py:113
  129.4 24.1 %all-to-all-done.2 = bf16[8,2,32,1024]{3,2,1,0:T(8,128)(2,1)} async-done(((bf16[8,2,32,1024]{3,2,1,0:T(8,128)(2,1)}), bf16[8,2,32,1024]{3,2,1,0:T(8,128)(2,1)}, u32[]{:S(2)}, u32[]{:S(2)}) %all-to-all-start.2) | async-done | bytes 1048608 | tf_op jit(solution)/shard_map/all_to_all | solution.py:113
  155.8 8.3 %fusion.14 = bf16[2048,2048]{1,0:T(8,128)(2,1)} fusion(bf16[1,1,512,2048]{3,2,1,0:T(8,128)(2,1)S(1)} %copy-done, bf16[512,1024]{0,1:T(8,128)(2,1)} %copy.263, bf16[512,1024]{0,1:T(8,128)(2,1)} %bitcast.319), kind=kOutput, calls=%fused_computation.29 | convolution fusion | flops 4299161600 | bytes 12582912 | tf_op jit(solution)/shard_map/dot_general | solution.py:117
  164.1 4.5 %fusion.18 = bf16[1024,512]{0,1:T(8,128)(2,1)S(1)} fusion(bf16[1,1,512,2048]{3,2,1,0:T(8,128)(2,1)S(1)} %copy-done, bf16[2048,2048]{1,0:T(8,128)(2,1)} %all-gather.2.cloned.1.call-done), kind=kOutput, calls=%fused_computation.39 | convolution fusion | flops 2148007936 | bytes 7340032 | tf_op jit(solution)/shard_map/dot_general | solution.py:123
  169.9 4.2 %all-to-all-start.5 = ((bf16[8,32,1024]{2,1,0:T(8,128)(2,1)}), bf16[8,32,1024]{2,1,0:T(8,128)(2,1)}, u32[]{:S(2)}, u32[]{:S(2)}) async-start(bf16[8,32,1024]{2,1,0:T(8,128)(2,1)} %get-tuple-element.36), calls=%async_computation.5 | async-start | bytes 1048576 | tf_op jit(solution)/shard_map/all_to_all | solution.py:133
  175.8 20.8 %all-to-all-done.5 = bf16[8,32,1024]{2,1,0:T(8,128)(2,1)} async-done(((bf16[8,32,1024]{2,1,0:T(8,128)(2,1)}), bf16[8,32,1024]{2,1,0:T(8,128)(2,1)}, u32[]{:S(2)}, u32[]{:S(2)}) %all-to-all-start.5) | async-done | bytes 524320 | tf_op jit(solution)/shard_map/all_to_all | solution.py:133
  196.6 4.1 %all-to-all-start.3 = ((bf16[8,32,1024]{2,1,0:T(8,128)(2,1)}), bf16[8,32,1024]{2,1,0:T(8,128)(2,1)}, u32[]{:S(2)}, u32[]{:S(2)}) async-start(bf16[8,32,1024]{2,1,0:T(8,128)(2,1)} %get-tuple-element.37), calls=%async_computation.3 | async-start | bytes 1048576 | tf_op jit(solution)/shard_map/all_to_all | solution.py:133
  200.8 4.6 %fusion.31 = bf16[64,8,8,128]{3,1,2,0:T(8,128)(2,1)S(1)} fusion(bf16[2048,2048]{1,0:T(8,128)(2,1)} %all-gather.2.cloned.1.call-done, bf16[1,1,512,2048]{3,2,1,0:T(8,128)(2,1)S(1)} %copy-done), kind=kOutput, calls=%fused_computation.42 | convolution fusion | flops 2148007936 | bytes 7340032 | tf_op jit(solution)/shard_map/dot_general | solution.py:119
  210.3 14.3 %all-to-all-done.3 = bf16[8,32,1024]{2,1,0:T(8,128)(2,1)} async-done(((bf16[8,32,1024]{2,1,0:T(8,128)(2,1)}), bf16[8,32,1024]{2,1,0:T(8,128)(2,1)}, u32[]{:S(2)}, u32[]{:S(2)}) %all-to-all-start.3) | async-done | bytes 524320 | tf_op jit(solution)/shard_map/all_to_all | solution.py:133
  249.8 4.7 %all-to-all-start.6 = ((bf16[8,3,1,32,1024]{4,3,1,2,0:T(8,128)(2,1)}), bf16[8,3,1,32,1024]{4,3,1,2,0:T(8,128)(2,1)}, u32[]{:S(2)}, u32[]{:S(2)}) async-start(bf16[8,3,1,32,1024]{4,3,1,2,0:T(8,128)(2,1)} %fusion.90), calls=%async_computation.6 | async-start | bytes 3145728 | tf_op jit(solution)/shard_map/all_to_all | solution.py:142
  264.5 46.5 %all-to-all-done.6 = bf16[8,3,1,32,1024]{4,3,1,2,0:T(8,128)(2,1)} async-done(((bf16[8,3,1,32,1024]{4,3,1,2,0:T(8,128)(2,1)}), bf16[8,3,1,32,1024]{4,3,1,2,0:T(8,128)(2,1)}, u32[]{:S(2)}, u32[]{:S(2)}) %all-to-all-start.6) | async-done | bytes 1572896 | tf_op jit(solution)/shard_map/all_to_all | solution.py:142
  311.1 6.2 %all-to-all-start.4 = ((bf16[8,3,1,32,1024]{4,3,1,2,0:T(8,128)(2,1)}), bf16[8,3,1,32,1024]{4,3,1,2,0:T(8,128)(2,1)}, u32[]{:S(2)}, u32[]{:S(2)}) async-start(bf16[8,3,1,32,1024]{4,3,1,2,0:T(8,128)(2,1)} %fusion.98), calls=%async_computation.4 | async-start | bytes 3145728 | tf_op jit(solution)/shard_map/all_to_all | solution.py:142
  317.3 5.1 %multiply_convert_fusion = bf16[8,512,512]{1,2,0:T(8,128)(2,1)S(1)} fusion(f32[8,512,512]{1,2,0:T(8,128)} %copy-done.2, f32[8,512]{1,0:T(8,128)S(1)} %multiply_reduce_fusion, f32[8,512]{1,0:T(8,128)S(1)} %bitcast.324, pred[512,512]{0,1:T(8,128)(4,1)S(1)} %fusion.53, bf16[512,8,128]{0,2,1:T(8,128)(2,1)S(1)} %copy-done.16, bf16[512,8,128]{0,2,1:T(8,128)(2,1)S(1)} %bitcast.289), kind=kOutput, calls=%fused_computation | convolution fusion | flops 547356672 | bytes 14974976 | tf_op jit(solution)/shard_map/ihd,jhd->hij/dot_general | solution.py:42
  325.0 4.0 %multiply_convert_fusion.1 = bf16[8,512,128]{1,2,0:T(8,128)(2,1)S(1)} fusion(bf16[8,512,512]{1,2,0:T(8,128)(2,1)} %copy-done.3, bf16[512,8,128]{0,2,1:T(8,128)(2,1)} %bitcast.299), kind=kOutput, calls=%fused_computation.33 | convolution fusion | flops 537919488 | bytes 6291456 | tf_op jit(solution)/shard_map/hij,ihd->jhd/dot_general | solution.py:45
  330.3 6.0 %fusion.28 = bf16[8,128,512]{2,1,0:T(8,128)(2,1)} fusion(bf16[512,8,128]{0,2,1:T(8,128)(2,1)S(1)} %copy-done.16, f32[8,512,512]{1,2,0:T(8,128)} %copy-done.2, f32[8,512]{1,0:T(8,128)S(1)} %bitcast.325, pred[512,512]{0,1:T(8,128)(4,1)S(1)} %fusion.53), kind=kOutput, calls=%fused_computation.41 | convolution fusion | flops 543686656 | bytes 10764288 | tf_op jit(solution)/shard_map/hij,ihd->jhd/dot_general | solution.py:39
  337.9 9.6 %fusion.12 = bf16[1,1,512,2048]{3,2,1,0:T(8,128)(2,1)} fusion(bf16[2048,2048]{1,0:T(8,128)(2,1)} %all-gather.2.cloned.1.call-done, bf16[512,1024]{0,1:T(8,128)(2,1)} %copy.263, bf16[512,1024]{0,1:T(8,128)(2,1)S(1)} %bitcast.320), kind=kOutput, calls=%fused_computation.23 | convolution fusion | flops 4300210176 | bytes 12582912 | tf_op jit(solution)/shard_map/dot_general | solution.py:168
  347.5 15.7 %all-to-all-done.4 = bf16[8,3,1,32,1024]{4,3,1,2,0:T(8,128)(2,1)} async-done(((bf16[8,3,1,32,1024]{4,3,1,2,0:T(8,128)(2,1)}), bf16[8,3,1,32,1024]{4,3,1,2,0:T(8,128)(2,1)}, u32[]{:S(2)}, u32[]{:S(2)}) %all-to-all-start.4) | async-done | bytes 1572896 | tf_op jit(solution)/shard_map/all_to_all | solution.py:142
  (195 shorter events, 103.3 us)
Async XLA Ops:
  7.2 148.6 %copy-start = (bf16[1,1,512,2048]{3,2,1,0:T(8,128)(2,1)S(1)}, bf16[1,1,512,2048]{3,2,1,0:T(8,128)(2,1)}, u32[]{:S(2)}) copy-start(bf16[1,1,512,2048]{3,2,1,0:T(8,128)(2,1)} %param.10) | copy-start | bytes 6291460
  7.2 156.9 %all-gather.2.cloned.1.call-start = ((), (), s32[]{:S(2)}) async-start(), calls=%async_computation.8 | async-start | bytes 10485760 | tf_op jit(solution)/shard_map/all_gather | solution.py:79
  16.5 6.5 %copy-start.43 = (s32[4,4]{1,0:T(4,128)S(1)}, s32[4,4]{1,0:T(4,128)}, u32[]{:S(2)}) copy-start(s32[4,4]{1,0:T(4,128)} %param.12) | copy-start | bytes 196
  16.5 6.6 %copy-start.42 = (s32[8,8]{1,0:T(8,128)S(1)}, s32[8,8]{1,0:T(8,128)}, u32[]{:S(2)}) copy-start(s32[8,8]{1,0:T(8,128)} %param.13) | copy-start | bytes 772
  16.5 44.4 %all-to-all-start.1 = ((bf16[3,8,32,1024]{3,2,0,1:T(8,128)(2,1)}), bf16[3,8,32,1024]{3,2,0,1:T(8,128)(2,1)}, u32[]{:S(2)}, u32[]{:S(2)}) async-start(bf16[3,8,32,1024]{3,2,0,1:T(8,128)(2,1)} %copy.256), calls=%async_computation.1 | async-start | bytes 3145728 | tf_op jit(solution)/shard_map/all_to_all | solution.py:89
  23.2 91.3 %copy-start.39 = (pred[8,8]{0,1:T(8,128)(4,1)}, pred[8,8]{0,1:T(8,128)(4,1)S(1)}, u32[]{:S(2)}) copy-start(pred[8,8]{0,1:T(8,128)(4,1)S(1)} %copy.250) | copy-start | bytes 196
  26.2 39.5 %copy-start.6 = (bf16[1,1,512,1024]{2,3,1,0:T(8,128)(2,1)}, bf16[1,1,512,1024]{2,3,1,0:T(8,128)(2,1)S(1)}, u32[]{:S(2)}) copy-start(bf16[1,1,512,1024]{2,3,1,0:T(8,128)(2,1)S(1)} %copy.339) | copy-start | bytes 3145732
  60.9 42.6 %all-to-all-start = ((bf16[3,8,32,1024]{3,2,0,1:T(8,128)(2,1)}), bf16[3,8,32,1024]{3,2,0,1:T(8,128)(2,1)}, u32[]{:S(2)}, u32[]{:S(2)}) async-start(bf16[3,8,32,1024]{3,2,0,1:T(8,128)(2,1)} %copy.248), calls=%async_computation | async-start | bytes 3145728 | tf_op jit(solution)/shard_map/all_to_all | solution.py:89
  107.0 7.5 %copy-start.37 = (f32[32,8,8]{2,1,0:T(8,128)}, f32[32,8,8]{2,1,0:T(8,128)S(1)}, u32[]{:S(2)}) copy-start(f32[32,8,8]{2,1,0:T(8,128)S(1)} %get-tuple-element.40) | copy-start | bytes 24580
  122.6 30.8 %all-to-all-start.2 = ((bf16[8,2,32,1024]{3,2,1,0:T(8,128)(2,1)}), bf16[8,2,32,1024]{3,2,1,0:T(8,128)(2,1)}, u32[]{:S(2)}, u32[]{:S(2)}) async-start(bf16[8,2,32,1024]{3,2,1,0:T(8,128)(2,1)} %copy.262), calls=%async_computation.2 | async-start | bytes 2097152 | tf_op jit(solution)/shard_map/all_to_all | solution.py:113
  126.9 243.0 %reduce-scatter.2.cloned.1.call-start = ((), (), s32[]{:S(2)}) async-start(), calls=%async_computation.9 | async-start | bytes 8650752 | tf_op jit(solution)/shard_map/reduce_scatter | solution.py:128
  169.9 26.7 %all-to-all-start.5 = ((bf16[8,32,1024]{2,1,0:T(8,128)(2,1)}), bf16[8,32,1024]{2,1,0:T(8,128)(2,1)}, u32[]{:S(2)}, u32[]{:S(2)}) async-start(bf16[8,32,1024]{2,1,0:T(8,128)(2,1)} %get-tuple-element.36), calls=%async_computation.5 | async-start | bytes 1048576 | tf_op jit(solution)/shard_map/all_to_all | solution.py:133
  196.6 27.9 %all-to-all-start.3 = ((bf16[8,32,1024]{2,1,0:T(8,128)(2,1)}), bf16[8,32,1024]{2,1,0:T(8,128)(2,1)}, u32[]{:S(2)}, u32[]{:S(2)}) async-start(bf16[8,32,1024]{2,1,0:T(8,128)(2,1)} %get-tuple-element.37), calls=%async_computation.3 | async-start | bytes 1048576 | tf_op jit(solution)/shard_map/all_to_all | solution.py:133
  208.3 17.4 %copy-start.5 = (f32[32,8,8,8]{2,3,1,0:T(8,128)S(1)}, f32[32,8,8,8]{2,3,1,0:T(8,128)}, u32[]{:S(2)}) copy-start(f32[32,8,8,8]{2,3,1,0:T(8,128)} %copy-done.4) | copy-start | bytes 196612
  234.4 3.5 copy-start.13
  238.0 3.5 copy-start.11
  249.8 4.8 %copy-start.26 = (bf16[32,8,128,8]{2,3,1,0:T(8,128)(2,1)S(1)}, bf16[32,8,128,8]{2,3,1,0:T(8,128)(2,1)}, u32[]{:S(2)}) copy-start(bf16[32,8,128,8]{2,3,1,0:T(8,128)(2,1)} %copy-done.25) | copy-start | bytes 1572868
  249.8 61.3 %all-to-all-start.6 = ((bf16[8,3,1,32,1024]{4,3,1,2,0:T(8,128)(2,1)}), bf16[8,3,1,32,1024]{4,3,1,2,0:T(8,128)(2,1)}, u32[]{:S(2)}, u32[]{:S(2)}) async-start(bf16[8,3,1,32,1024]{4,3,1,2,0:T(8,128)(2,1)} %fusion.90), calls=%async_computation.6 | async-start | bytes 3145728 | tf_op jit(solution)/shard_map/all_to_all | solution.py:142
  262.5 54.8 %copy-start.15 = (bf16[1,1,512,1024]{2,3,1,0:T(8,128)(2,1)S(1)}, bf16[1,1,512,1024]{2,3,1,0:T(8,128)(2,1)}, u32[]{:S(2)}) copy-start(bf16[1,1,512,1024]{2,3,1,0:T(8,128)(2,1)} %copy.340) | copy-start | bytes 3145732
  262.5 54.8 %copy-start.16 = (bf16[512,8,128]{0,2,1:T(8,128)(2,1)S(1)}, bf16[512,8,128]{0,2,1:T(8,128)(2,1)}, u32[]{:S(2)}) copy-start(bf16[512,8,128]{0,2,1:T(8,128)(2,1)} %copy.302) | copy-start | bytes 3145732
  262.5 54.8 %copy-start.38 = (f32[8,512,1]{1,0,2:T(8,128)S(1)}, f32[8,512,1]{1,0,2:T(8,128)}, u32[]{:S(2)}) copy-start(f32[8,512,1]{1,0,2:T(8,128)} %add_bitcast_fusion) | copy-start | bytes 49156
  311.1 52.2 %all-to-all-start.4 = ((bf16[8,3,1,32,1024]{4,3,1,2,0:T(8,128)(2,1)}), bf16[8,3,1,32,1024]{4,3,1,2,0:T(8,128)(2,1)}, u32[]{:S(2)}, u32[]{:S(2)}) async-start(bf16[8,3,1,32,1024]{4,3,1,2,0:T(8,128)(2,1)} %fusion.98), calls=%async_computation.4 | async-start | bytes 3145728 | tf_op jit(solution)/shard_map/all_to_all | solution.py:142
  317.3 5.1 %copy-start.7 = (bf16[1,1,512,1024]{2,3,1,0:T(8,128)(2,1)S(1)}, bf16[1,1,512,1024]{2,3,1,0:T(8,128)(2,1)}, u32[]{:S(2)}) copy-start(bf16[1,1,512,1024]{2,3,1,0:T(8,128)(2,1)} %copy-done.6) | copy-start | bytes 3145732
  368.4 3.3 copy-start.1
  (29 other events, 47.5 us)
Sparse Core Ops, SparseCore 0:
  9.9 90.2 all-gather.1
  164.3 175.4 reduce-scatter.1
